TPU v7x, 512 devices: a whole 4x4x16 slice. The times are simulated.
512 devices in a mesh: dp: 16 (over z), expert: 32 (over x, y, core).
Axes of the slice: x: 4, y: 4, z: 16, core: 2. Of those that a mesh axis runs over, the one named last changes fastest.
Arguments:
- x_tokens: bfloat16 [65536, 2048], P(('dp', 'expert')), may hold values from -6 to 6
- grad_out: bfloat16 [65536, 2048], P(('dp', 'expert')), may hold values from -6 to 6
- expert_ids: int32 [65536, 2], P(('dp', 'expert')), may hold values from 0 to 31, all different within a row; in each aligned block of 128 rows (0 to 127, 128 to 255, ...) at most 10 rows name the same one
- route_probs: float32 [65536, 2], P(('dp', 'expert')), may hold values from 0.1 to 1
- w_gate: bfloat16 [32, 2048, 768], P('expert', 'dp'), may hold values from -0.125 to 0.125
- w_up: bfloat16 [32, 2048, 768], P('expert', 'dp'), may hold values from -0.125 to 0.125
- w_down: bfloat16 [32, 2048, 768], P('expert', 'dp'), may hold values from -0.21875 to 0.21875
Outputs:
- grad_x: bfloat16 [65536, 2048], P(('dp', 'expert'))
- grad_probs: bfloat16 [65536, 2], P(('dp', 'expert'))
- grad_w_down: bfloat16 [32, 2048, 768], P('expert', 'dp')
Inputs may be any that keep to these rules, and one draw needn't show every extreme that they name: `expert_ids`: each token names 2 different experts; among the 128 tokens of one device no expert is named by more than 10 routes, and in every draw some device names some expert exactly 10 times.
All inputs are finite; a program needn't handle non-finite values.
Results may differ from a plain program's by a relative error of at most 0.017.
Values may be sent and summed in bfloat16 or wider, within the bound.
No kernel may reach another device: no remote copies, remote signals or barrier semaphores. Data moves between devices by JAX's collectives and lax.ppermute only.
A program may use at most 64 MiB of HBM per device.

v0:
```python
import jax
import jax.numpy as jnp
from jax import lax
from jax.sharding import PartitionSpec as P


def per_device(x_tokens, grad_out, expert_ids, route_probs, w_gate, w_up, w_down):
    tok_count, model_width = x_tokens.shape
    top_count = expert_ids.shape[1]
    n_expert = lax.axis_size("expert")
    capacity = tok_count * top_count * 5 // (4 * n_expert)
    slot_count = n_expert * capacity
    routes = tok_count * top_count
    flat_ids = expert_ids.reshape(routes)
    onehot = (flat_ids[:, None] == jnp.arange(n_expert, dtype=jnp.int32)).astype(jnp.int32)
    route_rank = jnp.sum((jnp.cumsum(onehot, axis=0) - onehot) * onehot, axis=1)
    target = flat_ids * capacity + route_rank
    source = (
        jnp.full((slot_count,), routes, jnp.int32)
        .at[target]
        .set(jnp.arange(routes, dtype=jnp.int32))
    )
    token_of = jnp.where(source < routes, source // top_count, tok_count)
    x_padded = jnp.concatenate([x_tokens, jnp.zeros((1, model_width), jnp.bfloat16)], axis=0)
    dy_padded = jnp.concatenate([grad_out, jnp.zeros((1, model_width), jnp.bfloat16)], axis=0)
    p_padded = jnp.concatenate([route_probs.reshape(routes), jnp.zeros((1,), jnp.float32)]).astype(
        jnp.bfloat16
    )
    x_slots = x_padded[token_of].reshape(n_expert, capacity, model_width)
    dy_slots = dy_padded[token_of].reshape(n_expert, capacity, model_width)
    p_slots = p_padded[source].reshape(n_expert, capacity)
    arrived = (
        lax.all_to_all(x_slots, "expert", split_axis=0, concat_axis=0, tiled=True),
        lax.all_to_all(dy_slots, "expert", split_axis=0, concat_axis=0, tiled=True),
        lax.all_to_all(p_slots, "expert", split_axis=0, concat_axis=0, tiled=True),
    )
    in_rows = arrived[0].reshape(slot_count, model_width)
    dy_rows = arrived[1].reshape(slot_count, model_width)
    p_rows = arrived[2].reshape(slot_count).astype(jnp.float32)
    scaled = (p_rows[:, None] * dy_rows.astype(jnp.float32)).astype(jnp.bfloat16)
    gate_full, up_full = (
        lax.all_gather(w_gate, "dp", axis=1, tiled=True),
        lax.all_gather(w_up, "dp", axis=1, tiled=True),
    )
    gate_full = gate_full[0]
    up_full = up_full[0]
    gate_pre = jnp.dot(in_rows, gate_full, preferred_element_type=jnp.float32)
    up_pre = jnp.dot(in_rows, up_full, preferred_element_type=jnp.float32)
    gate_sig = jax.nn.sigmoid(gate_pre)
    gate_act = gate_pre * gate_sig
    hidden = (gate_act * up_pre).astype(jnp.bfloat16)
    piece_rows = lax.all_gather(w_down, "dp", axis=1, tiled=True)[0]
    out_piece = jnp.dot(hidden, piece_rows.T, preferred_element_type=jnp.float32)
    grad_sum = jnp.dot(scaled, piece_rows, preferred_element_type=jnp.float32)
    prob_sum = jnp.sum(dy_rows.astype(jnp.float32) * out_piece, axis=1)
    hidden_grad, prob_sum = (grad_sum, prob_sum)
    up_grad = (hidden_grad * gate_act).astype(jnp.bfloat16)
    gate_grad = (hidden_grad * up_pre * gate_sig * (1.0 + gate_pre * (1.0 - gate_sig))).astype(
        jnp.bfloat16
    )
    x_grad = (
        jnp.dot(gate_grad, gate_full.T, preferred_element_type=jnp.float32)
        + jnp.dot(up_grad, up_full.T, preferred_element_type=jnp.float32)
    ).astype(jnp.bfloat16)
    down_grad = lax.psum_scatter(
        lax.dot_general(
            scaled, hidden, (((0,), (0,)), ((), ())), preferred_element_type=jnp.float32
        ).astype(jnp.bfloat16),
        "dp",
        scatter_dimension=0,
        tiled=True,
    )
    grad_w_down = down_grad[None]
    returned = (
        lax.all_to_all(
            x_grad.reshape(n_expert, capacity, model_width),
            "expert",
            split_axis=0,
            concat_axis=0,
            tiled=True,
        ),
        lax.all_to_all(
            prob_sum.astype(jnp.bfloat16).reshape(n_expert, capacity),
            "expert",
            split_axis=0,
            concat_axis=0,
            tiled=True,
        ),
    )
    grad_slots = returned[0].reshape(slot_count, model_width)
    prob_slots = returned[1].reshape(slot_count)
    picked = grad_slots[target].astype(jnp.float32).reshape(tok_count, top_count, model_width)
    grad_x = jnp.sum(picked, axis=1).astype(jnp.bfloat16)
    grad_probs = prob_slots[target].reshape(tok_count, top_count)
    return (grad_x, grad_probs, grad_w_down)


def solution(mesh):
    return jax.shard_map(
        per_device,
        mesh=mesh,
        in_specs=(
            P(("dp", "expert"), None),
            P(("dp", "expert"), None),
            P(("dp", "expert"), None),
            P(("dp", "expert"), None),
            P("expert", "dp", None),
            P("expert", "dp", None),
            P("expert", "dp", None),
        ),
        out_specs=(P(("dp", "expert"), None), P(("dp", "expert"), None), P("expert", "dp", None)),
        check_vma=False,
    )
```

profile of v0, /device:TPU:4, one launch (start us, length us, event | category | flops | bytes accessed | tf_op | source)
XLA Modules:
  0.0 322.4 jit_solution(13100136976467206266)
XLA Ops:
  13.3 1.4 scatter_custom_fusion
  14.8 2.5 gather_fusion
  18.0 9.4 %all-to-all-start = ((bf16[32,1,10]{2,1,0:T(2,128)(2,1)}), bf16[32,1,10]{2,1,0:T(2,128)(2,1)S(1)}, u32[]{:S(2)}, u32[]{:S(2)}) async-start(bf16[32,1,10]{2,1,0:T(2,128)(2,1)} %all_to_all.25), calls=%async_computation | async-start | bytes 32768 | tf_op jit(solution)/shard_map/all_to_all | solution.py:35
  27.5 2.4 gather_fusion.2
  29.9 1.7 reshape.123
  32.7 6.4 %all-to-all-start.2 = ((bf16[32,10,2048]{2,1,0:T(8,128)(2,1)}), bf16[32,10,2048]{2,1,0:T(8,128)(2,1)S(1)}, u32[]{:S(2)}, u32[]{:S(2)}) async-start(bf16[32,10,2048]{2,1,0:T(8,128)(2,1)} %reshape.123), calls=%async_computation.2 | async-start | bytes 4194304 | tf_op jit(solution)/shard_map/all_to_all | solution.py:33
  39.2 3.0 gather_fusion.1
  42.2 3.3 %reshape.122 = bf16[32,10,2048]{2,1,0:T(8,128)(2,1)} reshape(bf16[320,2048]{1,0:T(8,128)(2,1)} %gather_fusion.1) | data formatting | bytes 2621440 | tf_op jit(solution)/shard_map/reshape | solution.py:30
  45.6 19.5 %all-to-all-done.2 = bf16[32,10,2048]{2,1,0:T(8,128)(2,1)S(1)} async-done(((bf16[32,10,2048]{2,1,0:T(8,128)(2,1)}), bf16[32,10,2048]{2,1,0:T(8,128)(2,1)S(1)}, u32[]{:S(2)}, u32[]{:S(2)}) %all-to-all-start.2) | async-done | bytes 1310752 | tf_op jit(solution)/shard_map/all_to_all | solution.py:33
  65.0 7.7 %all-to-all-start.1 = ((bf16[32,10,2048]{2,1,0:T(8,128)(2,1)}), bf16[32,10,2048]{2,1,0:T(8,128)(2,1)}, u32[]{:S(2)}, u32[]{:S(2)}) async-start(bf16[32,10,2048]{2,1,0:T(8,128)(2,1)} %reshape.122), calls=%async_computation.1 | async-start | bytes 4194304 | tf_op jit(solution)/shard_map/all_to_all | solution.py:34
  73.1 1.4 reshape.124
  74.5 24.1 %all-to-all-done.1 = bf16[32,10,2048]{2,1,0:T(8,128)(2,1)} async-done(((bf16[32,10,2048]{2,1,0:T(8,128)(2,1)}), bf16[32,10,2048]{2,1,0:T(8,128)(2,1)}, u32[]{:S(2)}, u32[]{:S(2)}) %all-to-all-start.1) | async-done | bytes 1310752 | tf_op jit(solution)/shard_map/all_to_all | solution.py:34
  98.6 2.5 reshape.130
  101.1 4.4 %fusion.2 = f32[320,768]{1,0:T(8,128)} fusion(bf16[320,2048]{1,0:T(8,128)(2,1)} %reshape.124, bf16[1,2048,768]{2,1,0:T(8,128)(2,1)} %all-gather.8.cloned.1.call-done), kind=kOutput, calls=%fused_computation.10 | convolution fusion | flops 1006632960 | bytes 5439488 | tf_op jit(solution)/shard_map/dot_general | solution.py:47
  105.6 58.7 %all-gather.6.cloned.1.call-done = bf16[1,2048,768]{2,1,0:T(8,128)(2,1)} async-done(((bf16[1,128,768]{2,1,0:T(8,128)(2,1)}), bf16[1,2048,768]{2,1,0:T(8,128)(2,1)}) %all-gather.6.cloned.1.call-update) | async-done | bytes 3145744 | tf_op jit(solution)/shard_map/all_gather | solution.py:43
  164.3 4.7 %multiply_convert_fusion.3 = (bf16[320,768]{1,0:T(8,128)(2,1)S(1)}, f32[320,768]{1,0:T(8,128)}) fusion(f32[320,768]{1,0:T(8,128)} %fusion.2, bf16[320,2048]{1,0:T(8,128)(2,1)} %reshape.124, bf16[1,2048,768]{2,1,0:T(8,128)(2,1)} %all-gather.6.cloned.1.call-done), kind=kOutput, calls=%fused_computation.26 | convolution fusion | flops 1008107520 | bytes 6914048 | tf_op jit(solution)/shard_map/dot_general | solution.py:48
  169.0 3.6 %convolution_convert_fusion = bf16[2048,768]{1,0:T(8,128)(2,1)} fusion(bf16[320,768]{1,0:T(8,128)(2,1)S(1)} %get-tuple-element.11, f32[320,2048]{1,0:T(8,128)S(1)} %reshape.130, f32[320]{0:T(512)S(1)} %reshape.131), kind=kOutput, calls=%fused_computation.7 | convolution fusion | flops 1009516544 | bytes 6259968 | tf_op jit(solution)/shard_map/dot_general | solution.py:66
  172.6 3.3 %multiply_convert_fusion = bf16[32,10,2048]{2,1,0:T(8,128)(2,1)} fusion(f32[32,10]{1,0:T(8,128)S(1)} %bitcast.54, bf16[32,10,2048]{2,1,0:T(8,128)(2,1)} %all-to-all-done.1), kind=kLoop, calls=%fused_computation.6 | loop fusion | flops 1966080 | bytes 2622720 | tf_op jit(solution)/shard_map/convert_element_type | solution.py:40
  175.9 3.6 %convert_element_type.80 = bf16[320,2048]{1,0:T(8,128)(2,1)} reshape(bf16[32,10,2048]{2,1,0:T(8,128)(2,1)} %multiply_convert_fusion) | data formatting | bytes 2621440 | tf_op jit(solution)/shard_map/convert_element_type | solution.py:40
  179.5 59.1 %all-gather.4.cloned.1.call-done = bf16[1,2048,768]{2,1,0:T(8,128)(2,1)} async-done(((bf16[1,128,768]{2,1,0:T(8,128)(2,1)}), bf16[1,2048,768]{2,1,0:T(8,128)(2,1)}) %all-gather.4.cloned.1.call-update) | async-done | bytes 3145744 | tf_op jit(solution)/shard_map/all_gather | solution.py:52
  238.7 3.2 fusion.21
  242.6 7.4 %all-to-all-start.4 = ((bf16[32,1,10]{2,1,0:T(2,128)(2,1)}), bf16[32,1,10]{2,1,0:T(2,128)(2,1)S(1)}, u32[]{:S(2)}, u32[]{:S(2)}) async-start(bf16[32,1,10]{2,1,0:T(2,128)(2,1)} %convert_element_type.96), calls=%async_computation.4 | async-start | bytes 32768 | tf_op jit(solution)/shard_map/all_to_all | solution.py:82
  250.1 3.6 %fusion.10 = f32[320,768]{1,0:T(8,128)S(1)} fusion(bf16[320,2048]{1,0:T(8,128)(2,1)} %convert_element_type.80, bf16[1,2048,768]{2,1,0:T(8,128)(2,1)} %all-gather.4.cloned.1.call-done), kind=kOutput, calls=%fused_computation.18 | convolution fusion | flops 1006632960 | bytes 5439488 | tf_op jit(solution)/shard_map/dot_general | solution.py:54
  253.8 1.3 fusion
  255.8 1.2 fusion.18
  257.0 1.6 reshape.125
  258.6 7.4 %all-to-all-start.3 = ((bf16[32,10,2048]{2,1,0:T(8,128)(2,1)}), bf16[32,10,2048]{2,1,0:T(8,128)(2,1)S(1)}, u32[]{:S(2)}, u32[]{:S(2)}) async-start(bf16[32,10,2048]{2,1,0:T(8,128)(2,1)} %reshape.125), calls=%async_computation.3 | async-start | bytes 4194304 | tf_op jit(solution)/shard_map/all_to_all | solution.py:75
  266.2 1.9 gather_fusion.4
  268.9 23.0 %all-to-all-done.3 = bf16[32,10,2048]{2,1,0:T(8,128)(2,1)S(1)} async-done(((bf16[32,10,2048]{2,1,0:T(8,128)(2,1)}), bf16[32,10,2048]{2,1,0:T(8,128)(2,1)S(1)}, u32[]{:S(2)}, u32[]{:S(2)}) %all-to-all-start.3) | async-done | bytes 1310752 | tf_op jit(solution)/shard_map/all_to_all | solution.py:75
  292.4 1.4 gather_fusion.3
  294.5 3.6 %reduce_sum.34 = bf16[128,2048]{1,0:T(8,128)(2,1)} reduce(bf16[128,2,2048]{2,1,0:T(2,128)(2,1)S(1)} %gather.21, bf16[]{:T(256)} %constant.36.clone.1), dimensions={1}, to_apply=%region_4.5 | reduce | flops 262144 | bytes 1572866 | tf_op jit(solution)/shard_map/reduce_sum | solution.py:93
  298.1 17.8 %reduce-scatter.2.cloned.1.call-done = bf16[128,768]{1,0:T(8,128)(2,1)} async-done(((bf16[2048,768]{1,0:T(8,128)(2,1)}), bf16[128,768]{1,0:T(8,128)(2,1)}) %reduce-scatter.2.cloned.1.call-update) | async-done | bytes 196624 | tf_op jit(solution)/shard_map/reduce_scatter | solution.py:65
  (57 shorter events, 12.1 us)
Async XLA Ops:
  7.2 20.3 %copy-start = (bf16[128,2048]{1,0:T(8,128)(2,1)S(1)}, bf16[128,2048]{1,0:T(8,128)(2,1)}, u32[]{:S(2)}) copy-start(bf16[128,2048]{1,0:T(8,128)(2,1)} %param.7) | copy-start | bytes 1572868
  7.2 94.0 %all-gather.8.cloned.1.call-start = ((), (), s32[]{:S(2)}) async-start(), calls=%async_computation.8 | async-start | bytes 3342336 | tf_op jit(solution)/shard_map/all_gather | solution.py:42
  7.9 156.4 %all-gather.6.cloned.1.call-start = ((), (), s32[]{:S(2)}) async-start(), calls=%async_computation.7 | async-start | bytes 3342336 | tf_op jit(solution)/shard_map/all_gather | solution.py:43
  8.7 230.0 %all-gather.4.cloned.1.call-start = ((), (), s32[]{:S(2)}) async-start(), calls=%async_computation.6 | async-start | bytes 3342336 | tf_op jit(solution)/shard_map/all_gather | solution.py:52
  18.0 14.7 %all-to-all-start = ((bf16[32,1,10]{2,1,0:T(2,128)(2,1)}), bf16[32,1,10]{2,1,0:T(2,128)(2,1)S(1)}, u32[]{:S(2)}, u32[]{:S(2)}) async-start(bf16[32,1,10]{2,1,0:T(2,128)(2,1)} %all_to_all.25), calls=%async_computation | async-start | bytes 32768 | tf_op jit(solution)/shard_map/all_to_all | solution.py:35
  31.6 7.5 %copy-start.1 = (bf16[128,2048]{1,0:T(8,128)(2,1)S(1)}, bf16[128,2048]{1,0:T(8,128)(2,1)}, u32[]{:S(2)}) copy-start(bf16[128,2048]{1,0:T(8,128)(2,1)} %param.8) | copy-start | bytes 1572868
  32.7 32.4 %all-to-all-start.2 = ((bf16[32,10,2048]{2,1,0:T(8,128)(2,1)}), bf16[32,10,2048]{2,1,0:T(8,128)(2,1)S(1)}, u32[]{:S(2)}, u32[]{:S(2)}) async-start(bf16[32,10,2048]{2,1,0:T(8,128)(2,1)} %reshape.123), calls=%async_computation.2 | async-start | bytes 4194304 | tf_op jit(solution)/shard_map/all_to_all | solution.py:33
  65.0 33.6 %all-to-all-start.1 = ((bf16[32,10,2048]{2,1,0:T(8,128)(2,1)}), bf16[32,10,2048]{2,1,0:T(8,128)(2,1)}, u32[]{:S(2)}, u32[]{:S(2)}) async-start(bf16[32,10,2048]{2,1,0:T(8,128)(2,1)} %reshape.122), calls=%async_computation.1 | async-start | bytes 4194304 | tf_op jit(solution)/shard_map/all_to_all | solution.py:34
  72.7 243.2 %reduce-scatter.2.cloned.1.call-start = ((), (), s32[]{:S(2)}) async-start(), calls=%async_computation.9 | async-start | bytes 3342336 | tf_op jit(solution)/shard_map/reduce_scatter | solution.py:65
  242.6 16.0 %all-to-all-start.4 = ((bf16[32,1,10]{2,1,0:T(2,128)(2,1)}), bf16[32,1,10]{2,1,0:T(2,128)(2,1)S(1)}, u32[]{:S(2)}, u32[]{:S(2)}) async-start(bf16[32,1,10]{2,1,0:T(2,128)(2,1)} %convert_element_type.96), calls=%async_computation.4 | async-start | bytes 32768 | tf_op jit(solution)/shard_map/all_to_all | solution.py:82
  250.0 3.6 %copy-start.2 = (bf16[1,2048,768]{2,1,0:T(8,128)(2,1)S(1)}, bf16[1,2048,768]{2,1,0:T(8,128)(2,1)}, u32[]{:S(2)}) copy-start(bf16[1,2048,768]{2,1,0:T(8,128)(2,1)} %all-gather.8.cloned.1.call-done) | copy-start | bytes 9437188
  250.0 3.6 %copy-start.4 = (f32[320,768]{1,0:T(8,128)S(1)}, f32[320,768]{1,0:T(8,128)}, u32[]{:S(2)}) copy-start(f32[320,768]{1,0:T(8,128)} %fusion.2) | copy-start | bytes 2949124
  250.0 3.8 %copy-start.5 = (f32[320,768]{1,0:T(8,128)S(1)}, f32[320,768]{1,0:T(8,128)}, u32[]{:S(2)}) copy-start(f32[320,768]{1,0:T(8,128)} %get-tuple-element.12) | copy-start | bytes 2949124
  253.8 2.0 copy-start.3
  258.6 33.3 %all-to-all-start.3 = ((bf16[32,10,2048]{2,1,0:T(8,128)(2,1)}), bf16[32,10,2048]{2,1,0:T(8,128)(2,1)S(1)}, u32[]{:S(2)}, u32[]{:S(2)}) async-start(bf16[32,10,2048]{2,1,0:T(8,128)(2,1)} %reshape.125), calls=%async_computation.3 | async-start | bytes 4194304 | tf_op jit(solution)/shard_map/all_to_all | solution.py:75
Sparse Core Ops, SparseCore 0:
  10.1 79.8 all-gather.7
  92.0 72.2 all-gather.5
  166.4 72.2 all-gather.3
  241.9 73.9 reduce-scatter.1
where the time goes:
time: 323 us; the launch traced here: 322 us
  waiting for transfers between devices  205 us (63%)
  starting transfers between devices  38.7 us (12%)
  local copies, waits for them, and re-layouts  32.9 us (10%)
  matrix products  22.1 us (7%)
  between operations  14.1 us (4%)
  other arithmetic  9.22 us (3%)
    all_gather x1, waiting for transfers between devices, per_device(): piece_rows = lax.all_gather(w_down, 'dp', axis=1, tiled=True)[0]  59.1 us
    all_gather x1, waiting for transfers between devices, per_device(): lax.all_gather(w_up, 'dp', axis=1, tiled=True)  58.7 us
    all_to_all x1, waiting for transfers between devices, per_device(): lax.all_to_all(dy_slots, 'expert', split_axis=0, concat_axis=0, tiled=True)  24.1 us
    all_to_all x1, waiting for transfers between devices, per_device(): lax.all_to_all(x_grad.reshape(n_expert, capacity, model_width), 'expert',...  23 us
    all_to_all x1, waiting for transfers between devices, per_device(): lax.all_to_all(x_slots, 'expert', split_axis=0, concat_axis=0, tiled=True)  19.5 us
    reduce_scatter x1, waiting for transfers between devices, per_device(): lax.psum_scatter(lax.dot_general(scaled, hidden, (((0,), (0,)), ((), ()))...  17.8 us
    all_to_all x1, starting transfers between devices, per_device(): lax.all_to_all(p_slots, 'expert', split_axis=0, concat_axis=0, tiled=True)  9.43 us
    all_to_all x1, starting transfers between devices, per_device(): lax.all_to_all(dy_slots, 'expert', split_axis=0, concat_axis=0, tiled=True)  7.69 us
  transfers between devices with their start and end apart: 9, of which 7 were waited for; matrix products, arithmetic and copies ran while one was open for 19% of the time, Pallas kernels for 0%

commit v1 on v0

--- a/solution.py
+++ b/solution.py
@@ -1,7 +1,16 @@
+import functools
 import jax
 import jax.numpy as jnp
 from jax import lax
 from jax.sharding import PartitionSpec as P
+
+
+def step_on_patch_all(vec, ax_name):
+    state_now = jnp.concatenate([vec for _ in range(lax.axis_size(ax_name))], 1)
+    return lax.all_to_all(state_now, ax_name, 1, 1, tiled=True)
+
+
+feed_patch_up = functools.partial(step_on_patch_all, ax_name="dp")
 
 
 def per_device(x_tokens, grad_out, expert_ids, route_probs, w_gate, w_up, w_down):
@@ -49,7 +58,7 @@
     gate_sig = jax.nn.sigmoid(gate_pre)
     gate_act = gate_pre * gate_sig
     hidden = (gate_act * up_pre).astype(jnp.bfloat16)
-    piece_rows = lax.all_gather(w_down, "dp", axis=1, tiled=True)[0]
+    piece_rows = feed_patch_up(w_down)[0]
     out_piece = jnp.dot(hidden, piece_rows.T, preferred_element_type=jnp.float32)
     grad_sum = jnp.dot(scaled, piece_rows, preferred_element_type=jnp.float32)
     prob_sum = jnp.sum(dy_rows.astype(jnp.float32) * out_piece, axis=1)

time: 323 us -> 417 us (1.29)
  the two profiles are of different devices: /device:TPU:4 before, /device:TPU:1 now
where the time goes in v1:
time: 417 us; the launch traced here: 415 us
  waiting for transfers between devices  213 us (51%)
  local copies, waits for them, and re-layouts  71.4 us (17%)
  starting transfers between devices  50.6 us (12%)
  other arithmetic  42.4 us (10%)
  matrix products  24 us (6%)
  between operations  14.1 us (3%)
    all_gather x1, waiting for transfers between devices, per_device(): lax.all_gather(w_up, 'dp', axis=1, tiled=True)  163 us
    unnamed x1, other arithmetic  33.2 us
    unnamed x34, local copies, waits for them, and re-layouts  32.1 us
    all_to_all x1, waiting for transfers between devices, per_device(): lax.all_to_all(x_grad.reshape(n_expert, capacity, model_width), 'expert',...  25.4 us
    all_to_all x1, waiting for transfers between devices, per_device(): lax.all_to_all(x_slots, 'expert', split_axis=0, concat_axis=0, tiled=True)  20.8 us
    all_to_all x1, starting transfers between devices, step_on_patch_all(): return lax.all_to_all(state_now, ax_name, 1, 1, tiled=True)  13.1 us
    all_to_all x1, starting transfers between devices, per_device(): lax.all_to_all(p_slots, 'expert', split_axis=0, concat_axis=0, tiled=True)  10.3 us
    all_to_all x1, starting transfers between devices, per_device(): lax.all_to_all(prob_sum.astype(jnp.bfloat16).reshape(n_expert, capacity),...  9.36 us
  transfers between devices with their start and end apart: 9, of which 4 were waited for; matrix products, arithmetic and copies ran while one was open for 33% of the time, Pallas kernels for 0%

profile of v1, /device:TPU:1, one launch (start us, length us, event | category | flops | bytes accessed | tf_op | source)
XLA Modules:
  0.0 415.2 jit_solution(840052673569704727)
XLA Ops:
  11.8 1.4 scatter_custom_fusion
  13.3 2.5 gather_fusion
  16.5 10.3 %all-to-all-start = ((bf16[32,1,10]{2,1,0:T(2,128)(2,1)}), bf16[32,1,10]{2,1,0:T(2,128)(2,1)S(1)}, u32[]{:S(2)}, u32[]{:S(2)}) async-start(bf16[32,1,10]{2,1,0:T(2,128)(2,1)} %all_to_all.29), calls=%async_computation | async-start | bytes 32768 | tf_op jit(solution)/shard_map/all_to_all | solution.py:44
  27.9 2.4 gather_fusion.2
  30.4 1.6 reshape.123
  32.0 1.9 all-to-all-done
  33.8 5.7 %all-to-all-start.3 = ((bf16[32,10,2048]{2,1,0:T(8,128)(2,1)}), bf16[32,10,2048]{2,1,0:T(8,128)(2,1)}, u32[]{:S(2)}, u32[]{:S(2)}) async-start(bf16[32,10,2048]{2,1,0:T(8,128)(2,1)} %reshape.123), calls=%async_computation.3 | async-start | bytes 4194304 | tf_op jit(solution)/shard_map/all_to_all | solution.py:42
  39.6 2.4 gather_fusion.1
  42.1 1.6 reshape.122
  47.1 20.8 %all-to-all-done.3 = bf16[32,10,2048]{2,1,0:T(8,128)(2,1)} async-done(((bf16[32,10,2048]{2,1,0:T(8,128)(2,1)}), bf16[32,10,2048]{2,1,0:T(8,128)(2,1)}, u32[]{:S(2)}, u32[]{:S(2)}) %all-to-all-start.3) | async-done | bytes 1310752 | tf_op jit(solution)/shard_map/all_to_all | solution.py:42
  67.9 4.5 %all-to-all-start.1 = ((bf16[32,10,2048]{2,1,0:T(8,128)(2,1)}), bf16[32,10,2048]{2,1,0:T(8,128)(2,1)S(1)}, u32[]{:S(2)}, u32[]{:S(2)}) async-start(bf16[32,10,2048]{2,1,0:T(8,128)(2,1)} %reshape.122), calls=%async_computation.1 | async-start | bytes 4194304 | tf_op jit(solution)/shard_map/all_to_all | solution.py:43
  80.0 6.9 %copy.85 = bf16[1,2048,768]{2,0,1:T(2,128)(2,1)} copy(bf16[1,2048,768]{2,1,0:T(8,128)(2,1)} %constant_dynamic-update-slice_fusion) | data formatting | bytes 6291456 | tf_op jit(solution)/shard_map/concatenate | solution.py:9
  87.4 33.2 %reduce.8 = bf16[2048,768]{1,0:T(8,128)(2,1)} reduce(bf16[2048,1,768]{2,1,0:T(2,128)(2,1)} %bitcast.57, bf16[]{:T(256)} %broadcast.117), dimensions={1}, to_apply=%bitcast.56.reduce_sub_computation | reduce | bytes 6291458
  120.7 6.3 %reshape.194 = bf16[16,2,49152]{2,1,0:T(2,128)(2,1)} reshape(bf16[2048,768]{1,0:T(8,128)(2,1)} %reduce.8) | data formatting | bytes 6291456
  128.4 13.1 %all-to-all-start.2 = ((bf16[16,2,49152]{2,1,0:T(2,128)(2,1)}), bf16[16,2,49152]{2,1,0:T(2,128)(2,1)}, u32[]{:S(2)}, u32[]{:S(2)}) async-start(bf16[16,2,49152]{2,1,0:T(2,128)(2,1)} %reshape.194), calls=%async_computation.2 | async-start | bytes 6291456 | tf_op jit(solution)/shard_map/all_to_all | solution.py:10
  142.6 3.6 reshape.124
  146.2 2.5 reshape.130
  148.8 4.4 %fusion.6 = f32[320,768]{1,0:T(8,128)} fusion(bf16[320,2048]{1,0:T(8,128)(2,1)} %reshape.124, bf16[1,2048,768]{2,1,0:T(8,128)(2,1)} %all-gather.5.cloned.1.call-done), kind=kOutput, calls=%fused_computation.14 | convolution fusion | flops 1006632960 | bytes 5439488 | tf_op jit(solution)/shard_map/dot_general | solution.py:56
  153.2 163.1 %all-gather.3.cloned.1.call-done = bf16[1,2048,768]{2,1,0:T(8,128)(2,1)} async-done(((bf16[1,128,768]{2,1,0:T(8,128)(2,1)}), bf16[1,2048,768]{2,1,0:T(8,128)(2,1)}) %all-gather.3.cloned.1.call-update) | async-done | bytes 3145744 | tf_op jit(solution)/shard_map/all_gather | solution.py:52
  316.3 4.7 %multiply_convert_fusion.3 = (bf16[320,768]{1,0:T(8,128)(2,1)S(1)}, f32[320,768]{1,0:T(8,128)}) fusion(f32[320,768]{1,0:T(8,128)} %fusion.6, bf16[320,2048]{1,0:T(8,128)(2,1)} %reshape.124, bf16[1,2048,768]{2,1,0:T(8,128)(2,1)} %all-gather.3.cloned.1.call-done), kind=kOutput, calls=%fused_computation.28 | convolution fusion | flops 1008107520 | bytes 6914048 | tf_op jit(solution)/shard_map/dot_general | solution.py:57
  321.0 3.6 convolution_convert_fusion
  324.6 3.3 multiply_convert_fusion
  327.9 3.6 convert_element_type.80
  331.5 11.5 %reshape.195 = bf16[2048,1,768]{2,1,0:T(2,128)(2,1)} reshape(bf16[16,2,49152]{2,1,0:T(2,128)(2,1)} %all-to-all-done.2) | data formatting | bytes 6291456
  343.0 4.1 fusion.21
  347.9 9.4 %all-to-all-start.5 = ((bf16[32,1,10]{2,1,0:T(2,128)(2,1)}), bf16[32,1,10]{2,1,0:T(2,128)(2,1)S(1)}, u32[]{:S(2)}, u32[]{:S(2)}) async-start(bf16[32,1,10]{2,1,0:T(2,128)(2,1)} %convert_element_type.96), calls=%async_computation.5 | async-start | bytes 32768 | tf_op jit(solution)/shard_map/all_to_all | solution.py:91
  357.2 4.6 %fusion.2 = f32[320,768]{1,0:T(8,128)S(1)} fusion(bf16[320,2048]{1,0:T(8,128)(2,1)} %convert_element_type.80, bf16[1,2048,768]{2,0,1:T(2,128)(2,1)} %bitcast.59), kind=kOutput, calls=%fused_computation.10 | convolution fusion | flops 1006632960 | bytes 5439488 | tf_op jit(solution)/shard_map/dot_general | solution.py:63
  365.1 1.6 reshape.125
  366.7 7.4 %all-to-all-start.4 = ((bf16[32,10,2048]{2,1,0:T(8,128)(2,1)}), bf16[32,10,2048]{2,1,0:T(8,128)(2,1)S(1)}, u32[]{:S(2)}, u32[]{:S(2)}) async-start(bf16[32,10,2048]{2,1,0:T(8,128)(2,1)} %reshape.125), calls=%async_computation.4 | async-start | bytes 4194304 | tf_op jit(solution)/shard_map/all_to_all | solution.py:84
  374.3 1.9 gather_fusion.4
  377.0 25.4 %all-to-all-done.4 = bf16[32,10,2048]{2,1,0:T(8,128)(2,1)S(1)} async-done(((bf16[32,10,2048]{2,1,0:T(8,128)(2,1)}), bf16[32,10,2048]{2,1,0:T(8,128)(2,1)S(1)}, u32[]{:S(2)}, u32[]{:S(2)}) %all-to-all-start.4) | async-done | bytes 1310752 | tf_op jit(solution)/shard_map/all_to_all | solution.py:84
  405.0 3.6 reduce_sum.34
  (79 shorter events, 28.1 us)
Async XLA Ops:
  7.2 141.6 %all-gather.5.cloned.1.call-start = ((), (), s32[]{:S(2)}) async-start(), calls=%async_computation.8 | async-start | bytes 3342336 | tf_op jit(solution)/shard_map/all_gather | solution.py:51
  16.5 17.3 %all-to-all-start = ((bf16[32,1,10]{2,1,0:T(2,128)(2,1)}), bf16[32,1,10]{2,1,0:T(2,128)(2,1)S(1)}, u32[]{:S(2)}, u32[]{:S(2)}) async-start(bf16[32,1,10]{2,1,0:T(2,128)(2,1)} %all_to_all.29), calls=%async_computation | async-start | bytes 32768 | tf_op jit(solution)/shard_map/all_to_all | solution.py:44
  30.3 9.2 %copy-start.2 = (bf16[128,2048]{1,0:T(8,128)(2,1)S(1)}, bf16[128,2048]{1,0:T(8,128)(2,1)}, u32[]{:S(2)}) copy-start(bf16[128,2048]{1,0:T(8,128)(2,1)} %param.8) | copy-start | bytes 1572868
  33.8 34.1 %all-to-all-start.3 = ((bf16[32,10,2048]{2,1,0:T(8,128)(2,1)}), bf16[32,10,2048]{2,1,0:T(8,128)(2,1)}, u32[]{:S(2)}, u32[]{:S(2)}) async-start(bf16[32,10,2048]{2,1,0:T(8,128)(2,1)} %reshape.123), calls=%async_computation.3 | async-start | bytes 4194304 | tf_op jit(solution)/shard_map/all_to_all | solution.py:42
  42.0 1.6 copy-start
  67.9 59.1 %all-to-all-start.1 = ((bf16[32,10,2048]{2,1,0:T(8,128)(2,1)}), bf16[32,10,2048]{2,1,0:T(8,128)(2,1)S(1)}, u32[]{:S(2)}, u32[]{:S(2)}) async-start(bf16[32,10,2048]{2,1,0:T(8,128)(2,1)} %reshape.122), calls=%async_computation.1 | async-start | bytes 4194304 | tf_op jit(solution)/shard_map/all_to_all | solution.py:43
  127.0 1.4 copy-start.1
  128.4 203.1 %all-to-all-start.2 = ((bf16[16,2,49152]{2,1,0:T(2,128)(2,1)}), bf16[16,2,49152]{2,1,0:T(2,128)(2,1)}, u32[]{:S(2)}, u32[]{:S(2)}) async-start(bf16[16,2,49152]{2,1,0:T(2,128)(2,1)} %reshape.194), calls=%async_computation.2 | async-start | bytes 6291456 | tf_op jit(solution)/shard_map/all_to_all | solution.py:10
  141.5 174.8 %all-gather.3.cloned.1.call-start = ((), (), s32[]{:S(2)}) async-start(), calls=%async_computation.7 | async-start | bytes 3342336 | tf_op jit(solution)/shard_map/all_gather | solution.py:52
  142.2 266.4 %reduce-scatter.2.cloned.1.call-start = ((), (), s32[]{:S(2)}) async-start(), calls=%async_computation.9 | async-start | bytes 3342336 | tf_op jit(solution)/shard_map/reduce_scatter | solution.py:74
  347.9 18.8 %all-to-all-start.5 = ((bf16[32,1,10]{2,1,0:T(2,128)(2,1)}), bf16[32,1,10]{2,1,0:T(2,128)(2,1)S(1)}, u32[]{:S(2)}, u32[]{:S(2)}) async-start(bf16[32,1,10]{2,1,0:T(2,128)(2,1)} %convert_element_type.96), calls=%async_computation.5 | async-start | bytes 32768 | tf_op jit(solution)/shard_map/all_to_all | solution.py:91
  357.2 4.6 %copy-start.3 = (bf16[1,2048,768]{2,1,0:T(8,128)(2,1)S(1)}, bf16[1,2048,768]{2,1,0:T(8,128)(2,1)}, u32[]{:S(2)}) copy-start(bf16[1,2048,768]{2,1,0:T(8,128)(2,1)} %all-gather.5.cloned.1.call-done) | copy-start | bytes 9437188
  357.2 4.6 %copy-start.5 = (f32[320,768]{1,0:T(8,128)S(1)}, f32[320,768]{1,0:T(8,128)}, u32[]{:S(2)}) copy-start(f32[320,768]{1,0:T(8,128)} %fusion.6) | copy-start | bytes 2949124
  357.2 4.7 %copy-start.6 = (f32[320,768]{1,0:T(8,128)S(1)}, f32[320,768]{1,0:T(8,128)}, u32[]{:S(2)}) copy-start(f32[320,768]{1,0:T(8,128)} %get-tuple-element.18) | copy-start | bytes 2949124
  361.9 1.9 copy-start.4
  366.7 35.7 %all-to-all-start.4 = ((bf16[32,10,2048]{2,1,0:T(8,128)(2,1)}), bf16[32,10,2048]{2,1,0:T(8,128)(2,1)S(1)}, u32[]{:S(2)}, u32[]{:S(2)}) async-start(bf16[32,10,2048]{2,1,0:T(8,128)(2,1)} %reshape.125), calls=%async_computation.4 | async-start | bytes 4194304 | tf_op jit(solution)/shard_map/all_to_all | solution.py:84
Sparse Core Ops, SparseCore 0:
  10.0 72.0 all-gather.4
  144.4 171.8 all-gather.2
  324.7 67.8 reduce-scatter.1
